TPU v7x, 512 devices: a whole 4x4x16 slice. The times are simulated.
512 devices in a mesh: section: 2 (over core), expert: 32 (over z_lo, x), tensor: 8 (over y, z_hi).
Axes of the slice: x: 4, y: 4, z: 16 (z_hi: 2, z_lo: 8; z = z_hi * 8 + z_lo), core: 2. Of those that a mesh axis runs over, the one named last changes fastest.
Arguments:
- sent: bfloat16 [2, 4096, 4096], P('section', ('expert', 'tensor')), may hold values from -20 to 20
- norm_gain: float32 [2, 4096], P('section'), may hold values from 0.1 to 1.9
- router: bfloat16 [2, 4096, 32], P('section'), may hold values from -0.09375 to 0.09375
- w_in: bfloat16 [2, 32, 4096, 2048], P('section', 'expert', None, 'tensor'), may hold values from -0.09375 to 0.09375
- w_out: bfloat16 [2, 32, 2048, 4096], P('section', 'expert', 'tensor'), may hold values from -0.125 to 0.125
- expert_ids: int32 [2, 4096, 2], P('section', ('expert', 'tensor')), may hold values from 0 to 31, as said below
Outputs:
- handed: bfloat16 [2, 4096, 4096], P('section', ('expert', 'tensor'))
Inputs may be any that keep to these rules, and one draw needn't show every extreme that they name: `expert_ids`: each token names two different experts of the 32.
All inputs are finite; a program needn't handle non-finite values.
Results may differ from a plain program's by a relative error of at most 0.0054.
Values may be sent and summed in bfloat16 or wider, within the bound.
No kernel may reach another device: no remote copies, remote signals or barrier semaphores. Data moves between devices by JAX's collectives and lax.ppermute only.
A program may use at most 64 MiB of HBM per device.

v0:
```python
import jax
import jax.numpy as jnp
from jax import lax
from jax.sharding import Mesh
from jax.sharding import PartitionSpec as P


def passed_along(value, axis, steps):
    count = lax.axis_size(axis)
    pairs = [(source, (source + steps) % count) for source in range(count)]
    return lax.ppermute(value, axis, pairs)


def normalize(inputs, gain_row):
    widened = inputs.astype(jnp.float32)
    mean_sq = jnp.mean(widened * widened, axis=-1, keepdims=True)
    return (widened * lax.rsqrt(mean_sq + 1e-05) * gain_row).astype(jnp.bfloat16)


def route(normed, router_mat, expert_pick, tok_block, capacity):
    logits = jnp.dot(normed, router_mat, preferred_element_type=jnp.float32)
    experts = router_mat.shape[1]
    labels = jnp.arange(experts, dtype=jnp.int32)
    pair_hot = (expert_pick[:, :, None] == labels[None, None, :]).astype(jnp.float32)
    picked = jnp.sum(pair_hot * logits[:, None, :], axis=-1)
    squashed = jax.nn.sigmoid(picked)
    gate_vals = squashed / jnp.sum(squashed, axis=-1, keepdims=True)
    blocks = expert_pick.shape[0] // tok_block
    pair_order = jnp.transpose(expert_pick.reshape(blocks, tok_block, 2), (0, 2, 1)).reshape(
        blocks, 2 * tok_block
    )
    one_hot = (pair_order[:, :, None] == labels[None, None, :]).astype(jnp.int32)
    before = jnp.cumsum(one_hot, axis=1) - one_hot
    pair_ranks = jnp.sum(before * one_hot, axis=-1)
    pair_ranks = jnp.transpose(pair_ranks.reshape(blocks, 2, tok_block), (0, 2, 1)).reshape(-1, 2)
    is_kept = pair_ranks < capacity
    return (gate_vals, pair_ranks, is_kept)


def on_device(sent, norm_gain, router, w_in, w_out, expert_ids):
    arrived = passed_along(sent, "section", 1)[0]
    tok_count = arrived.shape[0]
    model_width = arrived.shape[1]
    experts = router.shape[2]
    top_count = expert_ids.shape[2]
    n_y = lax.axis_size("y")
    capacity = max(2, (5 * top_count * tok_count + 4 * experts - 1) // (4 * experts))
    normed = normalize(arrived, norm_gain[0])
    own_pick = expert_ids[0]
    partner_rows = passed_along(normed, "zh", 1)
    partner_pick = passed_along(own_pick, "zh", 1)
    rows_both = jnp.concatenate([normed, partner_rows], axis=0)
    pick_both = jnp.concatenate([own_pick, partner_pick], axis=0)
    gate_vals, pair_ranks, is_kept = route(rows_both, router[0], pick_both, tok_count, capacity)
    n_tok = 2 * tok_count
    block_of = (jnp.arange(n_tok, dtype=jnp.int32) // tok_count)[:, None]
    per_expert = 2 * capacity
    slot_ids = pick_both * per_expert + block_of * capacity + pair_ranks
    slot_count = experts * per_expert
    slot_labels = jnp.arange(slot_count, dtype=jnp.int32)
    slot_hot = ((slot_ids[:, :, None] == slot_labels[None, None, :]) & is_kept[:, :, None]).astype(
        jnp.float32
    )
    placement = jnp.transpose(jnp.sum(slot_hot, axis=1)).astype(jnp.bfloat16)
    combine_mat = jnp.sum(slot_hot * gate_vals[:, :, None], axis=1)
    send_rows = jnp.dot(placement, rows_both, preferred_element_type=jnp.float32).astype(
        jnp.bfloat16
    )
    slot_grid = send_rows.reshape(experts, per_expert, model_width)
    received = lax.all_to_all(slot_grid, "expert", split_axis=0, concat_axis=0, tiled=True)
    gathered = lax.all_gather(received[None], "y", axis=0, tiled=True)
    rows_in = gathered.reshape(-1, model_width)
    hidden = jax.nn.gelu(jnp.dot(rows_in, w_in[0, 0], preferred_element_type=jnp.float32)).astype(
        jnp.bfloat16
    )
    partial = jnp.dot(hidden, w_out[0, 0], preferred_element_type=jnp.float32).astype(jnp.bfloat16)
    summed = lax.psum_scatter(
        partial.reshape(n_y, -1, model_width), "y", scatter_dimension=0, tiled=True
    )
    back = lax.all_to_all(
        summed.reshape(experts, per_expert, model_width),
        "expert",
        split_axis=0,
        concat_axis=0,
        tiled=True,
    )
    half_sum = jnp.dot(
        combine_mat,
        back.reshape(slot_count, model_width).astype(jnp.float32),
        precision=lax.Precision.HIGHEST,
    )
    from_partner = passed_along(half_sum[tok_count:].astype(jnp.bfloat16), "zh", 1)
    combined = arrived.astype(jnp.float32) + half_sum[:tok_count] + from_partner.astype(jnp.float32)
    return passed_along(combined.astype(jnp.bfloat16)[None], "section", 1)


def solution(mesh):
    sizes = dict(mesh.shape)
    n_tensor = sizes["tensor"]
    fine = Mesh(
        mesh.devices.reshape(sizes["section"], sizes["expert"], n_tensor // 2, 2),
        ("section", "expert", "y", "zh"),
    )
    tokens = ("expert", "y", "zh")
    hidden_units = ("y", "zh")
    return jax.shard_map(
        on_device,
        mesh=fine,
        in_specs=(
            P("section", tokens, None),
            P("section", None),
            P("section", None, None),
            P("section", "expert", None, hidden_units),
            P("section", "expert", hidden_units, None),
            P("section", tokens, None),
        ),
        out_specs=P("section", tokens, None),
        check_vma=False,
    )
```

profile of v0, /device:TPU:3, one launch (start us, length us, event | category | flops | bytes accessed | tf_op | source)
XLA Modules:
  0.0 338.4 jit_solution(3203111217646648346)
XLA Ops:
  6.5 0.0 copy-start
  6.5 0.0 all-gather.3.cloned.1.call-start
  6.5 15.6 %collective-permute-start.1 = (s32[16,2]{0,1:T(2,128)}, s32[16,2]{0,1:T(2,128)S(1)}, u32[]{:S(2)}, u32[]{:S(2)}) collective-permute-start(s32[16,2]{0,1:T(2,128)} %bitcast.39), channel_id=1, source_target_pairs={{0,1},{1,0},{2,3},{3,2},{4,5},{5,4},{6,7},{7,6},{8,9},{9,8},{10,11... | collective-permute-start | bytes 392 | tf_op jit(solution)/shard_map/ppermute | solution.py:11
  22.1 2.9 collective-permute-start
  25.0 0.0 collective-permute-done.1
  25.0 0.8 pad_add_fusion
  25.8 0.1 reshape.115
  25.9 0.1 eq.20
  25.9 0.1 fusion.29
  26.0 0.1 reduce_window_sum.11
  26.1 0.2 select_reduce_fusion.2
  26.3 0.1 reshape.116
  26.3 0.1 reshape.117
  26.4 0.8 add_add_fusion
  27.2 0.0 collective-permute-done
  27.2 0.1 fusion.17
  27.4 0.8 fusion.19
  28.2 10.3 %collective-permute-start.2 = (bf16[16,4096]{1,0:T(8,128)(2,1)S(1)}, bf16[16,4096]{1,0:T(8,128)(2,1)S(1)}, u32[]{:S(2)}, u32[]{:S(2)}) collective-permute-start(bf16[16,4096]{1,0:T(8,128)(2,1)S(1)} %fusion.19), channel_id=1, source_target_pairs={{0,1},{1,0},{2,3},{3,2},{4,5},{5,4},{6,7},{7,6},{8,9},{9,8},{10,11... | collective-permute-start | bytes 393224 | tf_op jit(solution)/shard_map/ppermute | solution.py:11
  38.5 5.3 %collective-permute-done.2 = bf16[16,4096]{1,0:T(8,128)(2,1)S(1)} collective-permute-done((bf16[16,4096]{1,0:T(8,128)(2,1)S(1)}, bf16[16,4096]{1,0:T(8,128)(2,1)S(1)}, u32[]{:S(2)}, u32[]{:S(2)}) %collective-permute-start.2) | collective-permute-done | bytes 131104 | tf_op jit(solution)/shard_map/ppermute | solution.py:11
  43.8 1.1 fusion.22
  45.0 0.2 select_reduce_fusion.1
  45.2 0.1 convert_reduce_fusion
  45.3 0.5 convolution_convert_fusion.1
  45.8 1.2 reshape.118
  47.0 65.4 %all_to_all.10 = bf16[32,4,4096]{2,1,0:T(4,128)(2,1)} all-to-all(bf16[32,4,4096]{2,1,0:T(4,128)(2,1)} %reshape.118), channel_id=1, replica_groups=mesh['section'=2,'expert'=32,'y'=4,'zh'=2] {'expert'}, dimensions={0} | all-to-all | bytes 2097152 | tf_op jit(solution)/shard_map/all_to_all | solution.py:70
  112.4 0.0 all-gather.3.cloned.1.call-update
  112.4 0.0 reduce-scatter.2.cloned.1.call-start
  112.5 56.1 %all-gather.3.cloned.1.call-done = bf16[128,4,4096]{2,1,0:T(4,128)(2,1)} async-done(((bf16[32,4,4096]{2,1,0:T(4,128)(2,1)}), bf16[128,4,4096]{2,1,0:T(4,128)(2,1)}) %all-gather.3.cloned.1.call-update) | async-done | bytes 4194320 | tf_op jit(solution)/shard_map/all_gather | solution.py:71
  168.6 6.9 %reshape.119 = bf16[512,4096]{1,0:T(8,128)(2,1)} reshape(bf16[128,4,4096]{2,1,0:T(4,128)(2,1)} %all-gather.3.cloned.1.call-done) | data formatting | bytes 8388608 | tf_op jit(solution)/shard_map/reshape | solution.py:72
  175.5 0.0 copy-done
  175.5 9.3 %convolution_convert_fusion = bf16[512,4096]{1,0:T(8,128)(2,1)} fusion(bf16[1,1,256,4096]{3,2,1,0:T(8,128)(2,1)S(1)} %copy-done, bf16[512,4096]{1,0:T(8,128)(2,1)} %reshape.119, bf16[1,1,4096,256]{3,2,1,0:T(8,128)(2,1)} %param.9), kind=kOutput, calls=%fused_computation | convolution fusion | flops 2150760448 | bytes 12582912 | tf_op jit(solution)/shard_map/dot_general | solution.py:76
  184.8 0.0 reduce-scatter.2.cloned.1.call-update
  184.8 55.2 %reduce-scatter.2.cloned.1.call-done = bf16[1,128,4096]{2,1,0:T(8,128)(2,1)} async-done(((bf16[4,128,4096]{2,1,0:T(8,128)(2,1)}), bf16[1,128,4096]{2,1,0:T(8,128)(2,1)}) %reduce-scatter.2.cloned.1.call-update) | async-done | bytes 1048592 | tf_op jit(solution)/shard_map/reduce_scatter | solution.py:77
  240.0 1.5 reshape.121
  241.5 62.2 %all_to_all.11 = bf16[32,4,4096]{2,1,0:T(4,128)(2,1)} all-to-all(bf16[32,4,4096]{2,1,0:T(4,128)(2,1)S(1)} %reshape.121), channel_id=1, replica_groups=mesh['section'=2,'expert'=32,'y'=4,'zh'=2] {'expert'}, dimensions={0} | all-to-all | bytes 2097152 | tf_op jit(solution)/shard_map/all_to_all | solution.py:80
  303.7 1.3 reshape.122
  305.0 0.5 fusion.39
  305.6 5.0 %collective-permute-start.3 = (bf16[16,4096]{1,0:T(8,128)(2,1)S(1)}, bf16[16,4096]{1,0:T(8,128)(2,1)S(1)}, u32[]{:S(2)}, u32[]{:S(2)}) collective-permute-start(bf16[16,4096]{1,0:T(8,128)(2,1)S(1)} %slice.15), channel_id=1, source_target_pairs={{0,1},{1,0},{2,3},{3,2},{4,5},{5,4},{6,7},{7,6},{8,9},{9,8},{10,11... | collective-permute-start | bytes 393224 | tf_op jit(solution)/shard_map/ppermute | solution.py:11
  310.6 16.9 %collective-permute-done.3 = bf16[16,4096]{1,0:T(8,128)(2,1)S(1)} collective-permute-done((bf16[16,4096]{1,0:T(8,128)(2,1)S(1)}, bf16[16,4096]{1,0:T(8,128)(2,1)S(1)}, u32[]{:S(2)}, u32[]{:S(2)}) %collective-permute-start.3) | collective-permute-done | bytes 131104 | tf_op jit(solution)/shard_map/ppermute | solution.py:11
  327.5 0.1 fusion.28
  327.5 2.4 collective-permute-start.4
  330.0 1.0 collective-permute-done.4
  331.0 0.7 copy.20
  (8 shorter events, 0.1 us)
Async XLA Ops:
  6.5 169.0 %copy-start = (bf16[1,1,256,4096]{3,2,1,0:T(8,128)(2,1)S(1)}, bf16[1,1,256,4096]{3,2,1,0:T(8,128)(2,1)}, u32[]{:S(2)}) copy-start(bf16[1,1,256,4096]{3,2,1,0:T(8,128)(2,1)} %param.10) | copy-start | bytes 6291460
  6.5 162.0 %all-gather.3.cloned.1.call-start = ((), (), s32[]{:S(2)}) async-start(), calls=%async_computation.4 | async-start | bytes 5242880 | tf_op jit(solution)/shard_map/all_gather | solution.py:71
  6.5 18.5 %collective-permute-start.1 = (s32[16,2]{0,1:T(2,128)}, s32[16,2]{0,1:T(2,128)S(1)}, u32[]{:S(2)}, u32[]{:S(2)}) collective-permute-start(s32[16,2]{0,1:T(2,128)} %bitcast.39), channel_id=1, source_target_pairs={{0,1},{1,0},{2,3},{3,2},{4,5},{5,4},{6,7},{7,6},{8,9},{9,8},{10,11... | collective-permute-start | bytes 392 | tf_op jit(solution)/shard_map/ppermute | solution.py:11
  22.1 5.1 %collective-permute-start = (bf16[1,16,4096]{2,1,0:T(8,128)(2,1)}, bf16[1,16,4096]{2,1,0:T(8,128)(2,1)S(1)}, u32[]{:S(2)}, u32[]{:S(2)}) collective-permute-start(bf16[1,16,4096]{2,1,0:T(8,128)(2,1)} %param.6), channel_id=1, source_target_pairs={{0,256},{256,0},{1,257},{257,1},{2,258},{258,2},{3,259},{259,3},{4... | collective-permute-start | bytes 393224 | tf_op jit(solution)/shard_map/ppermute | solution.py:11
  28.2 15.7 %collective-permute-start.2 = (bf16[16,4096]{1,0:T(8,128)(2,1)S(1)}, bf16[16,4096]{1,0:T(8,128)(2,1)S(1)}, u32[]{:S(2)}, u32[]{:S(2)}) collective-permute-start(bf16[16,4096]{1,0:T(8,128)(2,1)S(1)} %fusion.19), channel_id=1, source_target_pairs={{0,1},{1,0},{2,3},{3,2},{4,5},{5,4},{6,7},{7,6},{8,9},{9,8},{10,11... | collective-permute-start | bytes 393224 | tf_op jit(solution)/shard_map/ppermute | solution.py:11
  112.4 127.6 %reduce-scatter.2.cloned.1.call-start = ((), (), s32[]{:S(2)}) async-start(), calls=%async_computation.3 | async-start | bytes 5242880 | tf_op jit(solution)/shard_map/reduce_scatter | solution.py:77
  305.6 21.9 %collective-permute-start.3 = (bf16[16,4096]{1,0:T(8,128)(2,1)S(1)}, bf16[16,4096]{1,0:T(8,128)(2,1)S(1)}, u32[]{:S(2)}, u32[]{:S(2)}) collective-permute-start(bf16[16,4096]{1,0:T(8,128)(2,1)S(1)} %slice.15), channel_id=1, source_target_pairs={{0,1},{1,0},{2,3},{3,2},{4,5},{5,4},{6,7},{7,6},{8,9},{9,8},{10,11... | collective-permute-start | bytes 393224 | tf_op jit(solution)/shard_map/ppermute | solution.py:11
  327.5 3.4 %collective-permute-start.4 = (bf16[1,16,4096]{2,1,0:T(8,128)(2,1)S(1)}, bf16[1,16,4096]{2,1,0:T(8,128)(2,1)S(1)}, u32[]{:S(2)}, u32[]{:S(2)}) collective-permute-start(bf16[1,16,4096]{2,1,0:T(8,128)(2,1)S(1)} %fusion.28), channel_id=1, source_target_pairs={{0,256},{256,0},{1,257},{257,1},{2,258},{258,2},{3,259},{259,3},{4... | collective-permute-start | bytes 393224 | tf_op jit(solution)/shard_map/ppermute | solution.py:11
Sparse Core Ops, SparseCore 0:
  112.6 55.9 all-gather.2
  184.9 55.0 reduce-scatter.1
where the time goes:
time: 339 us; the launch traced here: 338 us
  waiting for transfers between devices  134 us (40%)
  blocking collectives  128 us (38%)
  starting transfers between devices  36.3 us (11%)
  between operations  13.5 us (4%)
  local copies, waits for them, and re-layouts  11.9 us (4%)
  matrix products  11.4 us (3%)
    all_to_all x1, blocking collectives, on_device(): lax.all_to_all(slot_grid, 'expert', split_axis=0, concat_axis=0, tiled=True)  65.4 us
    all_to_all x1, blocking collectives, on_device(): lax.all_to_all(summed.reshape(experts, per_expert, model_width), 'expert'...  62.2 us
    all_gather x1, waiting for transfers between devices, on_device(): gathered = lax.all_gather(received[None], 'y', axis=0, tiled=True)  56.1 us
    reduce_scatter x1, waiting for transfers between devices, on_device(): lax.psum_scatter(partial.reshape(n_y, -1, model_width), 'y', scatter_dime...  55.2 us
    ppermute x5, starting transfers between devices, passed_along(): return lax.ppermute(value, axis, pairs)  36.2 us
    ppermute x5, waiting for transfers between devices, passed_along(): return lax.ppermute(value, axis, pairs)  23.1 us
    dot_general x1, matrix products, on_device(): jnp.dot(hidden, w_out[0, 0], preferred_element_type=jnp.float32)  9.31 us
    reshape x1, local copies, waits for them, and re-layouts, on_device(): rows_in = gathered.reshape(-1, model_width)  6.91 us
  transfers between devices with their start and end apart: 7, of which 5 were waited for; matrix products, arithmetic and copies ran while one was open for 1% of the time, Pallas kernels for 0%

commit v1 on v0

--- a/solution.py
+++ b/solution.py
@@ -68,7 +68,11 @@
     )
     slot_grid = send_rows.reshape(experts, per_expert, model_width)
     received = lax.all_to_all(slot_grid, "expert", split_axis=0, concat_axis=0, tiled=True)
-    gathered = lax.all_gather(received[None], "y", axis=0, tiled=True)
+    block = received[None]
+    size = lax.axis_size("y")
+    tiles = jnp.stack([block for _ in range(size)])
+    tiles = lax.all_to_all(tiles, "y", split_axis=0, concat_axis=0)
+    gathered = jnp.concatenate(tiles, axis=0)
     rows_in = gathered.reshape(-1, model_width)
     hidden = jax.nn.gelu(jnp.dot(rows_in, w_in[0, 0], preferred_element_type=jnp.float32)).astype(
         jnp.bfloat16

time: 339 us -> 335 us (0.988)
  waiting for transfers between devices: 134 us -> 77.8 us
  blocking collectives: 128 us -> 178 us
    all_gather x1 -> x0, waiting for transfers between devices: 56.1 us -> none  [on_device(): gathered = lax.all_gather(received[None], 'y', axis=0, tiled=True)]
    all_to_all x0 -> x1, blocking collectives: none -> 50.4 us  [on_device(): tiles = lax.all_to_all(tiles, 'y', split_axis=0, concat_axis=0)]
    another operation x0 -> x2, local copies, waits for them, and re-layouts: none -> 9.01 us  [the longest x1 6.92 us: on_device(): rows_in = gathered.reshape(-1, model_width)]
    reshape x1 -> x0, local copies, waits for them, and re-layouts: 6.91 us -> none  [on_device(): rows_in = gathered.reshape(-1, model_width)]
  transfers between devices with their start and end apart: 7 -> 6, of which waited for: 5 -> 4; matrix products, arithmetic and copies ran while one was open for 1% -> 1% of each run, Pallas kernels for 0% -> 0%
where the time goes in v1:
time: 335 us; the launch traced here: 334 us
  blocking collectives  178 us (53%)
  waiting for transfers between devices  77.8 us (23%)
  starting transfers between devices  36.2 us (11%)
  local copies, waits for them, and re-layouts  14 us (4%)
  between operations  13.5 us (4%)
  matrix products  11.5 us (3%)
    all_to_all x1, blocking collectives, on_device(): lax.all_to_all(slot_grid, 'expert', split_axis=0, concat_axis=0, tiled=True)  65.3 us
    all_to_all x1, blocking collectives, on_device(): lax.all_to_all(summed.reshape(experts, per_expert, model_width), 'expert'...  62.2 us
    reduce_scatter x1, waiting for transfers between devices, on_device(): lax.psum_scatter(partial.reshape(n_y, -1, model_width), 'y', scatter_dime...  54.6 us
    all_to_all x1, blocking collectives, on_device(): tiles = lax.all_to_all(tiles, 'y', split_axis=0, concat_axis=0)  50.4 us
    ppermute x5, starting transfers between devices, passed_along(): return lax.ppermute(value, axis, pairs)  36.2 us
    ppermute x5, waiting for transfers between devices, passed_along(): return lax.ppermute(value, axis, pairs)  23.1 us
    dot_general x1, matrix products, on_device(): jnp.dot(hidden, w_out[0, 0], preferred_element_type=jnp.float32)  9.35 us
    another operation x1, local copies, waits for them, and re-layouts, on_device(): rows_in = gathered.reshape(-1, model_width)  6.92 us
  transfers between devices with their start and end apart: 6, of which 4 were waited for; matrix products, arithmetic and copies ran while one was open for 1% of the time, Pallas kernels for 0%

profile of v1, /device:TPU:3, one launch (start us, length us, event | category | flops | bytes accessed | tf_op | source)
XLA Modules:
  0.0 334.1 jit_solution(5333682980645637386)
XLA Ops:
  6.5 0.0 copy-start
  6.5 0.0 reduce-scatter.2.cloned.1.call-start
  6.5 15.6 %collective-permute-start.1 = (s32[16,2]{0,1:T(2,128)}, s32[16,2]{0,1:T(2,128)S(1)}, u32[]{:S(2)}, u32[]{:S(2)}) collective-permute-start(s32[16,2]{0,1:T(2,128)} %bitcast.39), channel_id=1, source_target_pairs={{0,1},{1,0},{2,3},{3,2},{4,5},{5,4},{6,7},{7,6},{8,9},{9,8},{10,11... | collective-permute-start | bytes 392 | tf_op jit(solution)/shard_map/ppermute | solution.py:11
  22.1 2.9 collective-permute-start
  25.0 0.0 collective-permute-done.1
  25.0 0.8 pad_add_fusion
  25.8 0.1 reshape.114
  25.9 0.1 eq.20
  25.9 0.1 fusion.29
  26.0 0.1 reduce_window_sum.11
  26.1 0.2 select_reduce_fusion.2
  26.3 0.1 reshape.115
  26.3 0.1 reshape.116
  26.4 0.8 add_add_fusion
  27.2 0.0 collective-permute-done
  27.2 0.1 fusion.17
  27.4 0.8 fusion.19
  28.2 10.3 %collective-permute-start.2 = (bf16[16,4096]{1,0:T(8,128)(2,1)S(1)}, bf16[16,4096]{1,0:T(8,128)(2,1)S(1)}, u32[]{:S(2)}, u32[]{:S(2)}) collective-permute-start(bf16[16,4096]{1,0:T(8,128)(2,1)S(1)} %fusion.19), channel_id=1, source_target_pairs={{0,1},{1,0},{2,3},{3,2},{4,5},{5,4},{6,7},{7,6},{8,9},{9,8},{10,11... | collective-permute-start | bytes 393224 | tf_op jit(solution)/shard_map/ppermute | solution.py:11
  38.5 5.3 %collective-permute-done.2 = bf16[16,4096]{1,0:T(8,128)(2,1)S(1)} collective-permute-done((bf16[16,4096]{1,0:T(8,128)(2,1)S(1)}, bf16[16,4096]{1,0:T(8,128)(2,1)S(1)}, u32[]{:S(2)}, u32[]{:S(2)}) %collective-permute-start.2) | collective-permute-done | bytes 131104 | tf_op jit(solution)/shard_map/ppermute | solution.py:11
  43.8 1.1 fusion.22
  45.0 0.2 select_reduce_fusion.1
  45.2 0.1 convert_reduce_fusion
  45.3 0.5 convolution_convert_fusion.1
  45.8 1.2 reshape.117
  47.0 65.3 %all_to_all.15 = bf16[32,4,4096]{2,1,0:T(4,128)(2,1)S(1)} all-to-all(bf16[32,4,4096]{2,1,0:T(4,128)(2,1)} %reshape.117), channel_id=1, replica_groups=mesh['section'=2,'expert'=32,'y'=4,'zh'=2] {'expert'}, dimensions={0} | all-to-all | bytes 2097152 | tf_op jit(solution)/shard_map/all_to_all | solution.py:70
  112.3 2.1 stack.3
  114.4 50.4 %all_to_all.16 = bf16[4,1,32,4,4096]{4,3,2,1,0:T(4,128)(2,1)} all-to-all(bf16[4,1,32,4,4096]{4,3,2,1,0:T(4,128)(2,1)S(1)} %stack.3), channel_id=1, replica_groups=mesh['section'=2,'expert'=32,'y'=4,'zh'=2] {'y'}, dimensions={0} | all-to-all | bytes 8388608 | tf_op jit(solution)/shard_map/all_to_all | solution.py:74
  164.8 6.9 %reshape_reshape.3 = bf16[512,4096]{1,0:T(8,128)(2,1)} reshape(bf16[4,1,32,4,4096]{4,3,2,1,0:T(4,128)(2,1)} %all_to_all.16) | data formatting | bytes 8388608 | tf_op jit(solution)/shard_map/reshape;reshape | solution.py:76
  171.7 0.0 copy-done
  171.7 9.4 %convolution_convert_fusion = bf16[512,4096]{1,0:T(8,128)(2,1)} fusion(bf16[1,1,256,4096]{3,2,1,0:T(8,128)(2,1)S(1)} %copy-done, bf16[512,4096]{1,0:T(8,128)(2,1)} %reshape_reshape.3, bf16[1,1,4096,256]{3,2,1,0:T(8,128)(2,1)} %param.9), kind=kOutput, calls=%fused_computation | convolution fusion | flops 2150760448 | bytes 12582912 | tf_op jit(solution)/shard_map/dot_general | solution.py:80
  181.0 0.0 reduce-scatter.2.cloned.1.call-update
  181.1 54.6 %reduce-scatter.2.cloned.1.call-done = bf16[1,128,4096]{2,1,0:T(8,128)(2,1)} async-done(((bf16[4,128,4096]{2,1,0:T(8,128)(2,1)}), bf16[1,128,4096]{2,1,0:T(8,128)(2,1)}) %reduce-scatter.2.cloned.1.call-update) | async-done | bytes 1048592 | tf_op jit(solution)/shard_map/reduce_scatter | solution.py:81
  235.7 1.5 reshape.119
  237.2 62.2 %all_to_all.17 = bf16[32,4,4096]{2,1,0:T(4,128)(2,1)} all-to-all(bf16[32,4,4096]{2,1,0:T(4,128)(2,1)S(1)} %reshape.119), channel_id=1, replica_groups=mesh['section'=2,'expert'=32,'y'=4,'zh'=2] {'expert'}, dimensions={0} | all-to-all | bytes 2097152 | tf_op jit(solution)/shard_map/all_to_all | solution.py:84
  299.4 1.3 reshape.120
  300.7 0.5 fusion.39
  301.3 5.0 %collective-permute-start.3 = (bf16[16,4096]{1,0:T(8,128)(2,1)S(1)}, bf16[16,4096]{1,0:T(8,128)(2,1)S(1)}, u32[]{:S(2)}, u32[]{:S(2)}) collective-permute-start(bf16[16,4096]{1,0:T(8,128)(2,1)S(1)} %slice.15), channel_id=1, source_target_pairs={{0,1},{1,0},{2,3},{3,2},{4,5},{5,4},{6,7},{7,6},{8,9},{9,8},{10,11... | collective-permute-start | bytes 393224 | tf_op jit(solution)/shard_map/ppermute | solution.py:11
  306.3 16.9 %collective-permute-done.3 = bf16[16,4096]{1,0:T(8,128)(2,1)S(1)} collective-permute-done((bf16[16,4096]{1,0:T(8,128)(2,1)S(1)}, bf16[16,4096]{1,0:T(8,128)(2,1)S(1)}, u32[]{:S(2)}, u32[]{:S(2)}) %collective-permute-start.3) | collective-permute-done | bytes 131104 | tf_op jit(solution)/shard_map/ppermute | solution.py:11
  323.1 0.1 fusion.28
  323.2 2.4 collective-permute-start.4
  325.6 1.0 collective-permute-done.4
  326.6 0.7 copy.15
  (8 shorter events, 0.1 us)
Async XLA Ops:
  6.5 165.2 %copy-start = (bf16[1,1,256,4096]{3,2,1,0:T(8,128)(2,1)S(1)}, bf16[1,1,256,4096]{3,2,1,0:T(8,128)(2,1)}, u32[]{:S(2)}) copy-start(bf16[1,1,256,4096]{3,2,1,0:T(8,128)(2,1)} %param.10) | copy-start | bytes 6291460
  6.5 229.2 %reduce-scatter.2.cloned.1.call-start = ((), (), s32[]{:S(2)}) async-start(), calls=%async_computation.4 | async-start | bytes 5242880 | tf_op jit(solution)/shard_map/reduce_scatter | solution.py:81
  6.5 18.5 %collective-permute-start.1 = (s32[16,2]{0,1:T(2,128)}, s32[16,2]{0,1:T(2,128)S(1)}, u32[]{:S(2)}, u32[]{:S(2)}) collective-permute-start(s32[16,2]{0,1:T(2,128)} %bitcast.39), channel_id=1, source_target_pairs={{0,1},{1,0},{2,3},{3,2},{4,5},{5,4},{6,7},{7,6},{8,9},{9,8},{10,11... | collective-permute-start | bytes 392 | tf_op jit(solution)/shard_map/ppermute | solution.py:11
  22.1 5.1 %collective-permute-start = (bf16[1,16,4096]{2,1,0:T(8,128)(2,1)}, bf16[1,16,4096]{2,1,0:T(8,128)(2,1)S(1)}, u32[]{:S(2)}, u32[]{:S(2)}) collective-permute-start(bf16[1,16,4096]{2,1,0:T(8,128)(2,1)} %param.6), channel_id=1, source_target_pairs={{0,256},{256,0},{1,257},{257,1},{2,258},{258,2},{3,259},{259,3},{4... | collective-permute-start | bytes 393224 | tf_op jit(solution)/shard_map/ppermute | solution.py:11
  28.2 15.7 %collective-permute-start.2 = (bf16[16,4096]{1,0:T(8,128)(2,1)S(1)}, bf16[16,4096]{1,0:T(8,128)(2,1)S(1)}, u32[]{:S(2)}, u32[]{:S(2)}) collective-permute-start(bf16[16,4096]{1,0:T(8,128)(2,1)S(1)} %fusion.19), channel_id=1, source_target_pairs={{0,1},{1,0},{2,3},{3,2},{4,5},{5,4},{6,7},{7,6},{8,9},{9,8},{10,11... | collective-permute-start | bytes 393224 | tf_op jit(solution)/shard_map/ppermute | solution.py:11
  301.3 21.9 %collective-permute-start.3 = (bf16[16,4096]{1,0:T(8,128)(2,1)S(1)}, bf16[16,4096]{1,0:T(8,128)(2,1)S(1)}, u32[]{:S(2)}, u32[]{:S(2)}) collective-permute-start(bf16[16,4096]{1,0:T(8,128)(2,1)S(1)} %slice.15), channel_id=1, source_target_pairs={{0,1},{1,0},{2,3},{3,2},{4,5},{5,4},{6,7},{7,6},{8,9},{9,8},{10,11... | collective-permute-start | bytes 393224 | tf_op jit(solution)/shard_map/ppermute | solution.py:11
  323.2 3.4 %collective-permute-start.4 = (bf16[1,16,4096]{2,1,0:T(8,128)(2,1)S(1)}, bf16[1,16,4096]{2,1,0:T(8,128)(2,1)S(1)}, u32[]{:S(2)}, u32[]{:S(2)}) collective-permute-start(bf16[1,16,4096]{2,1,0:T(8,128)(2,1)S(1)} %fusion.28), channel_id=1, source_target_pairs={{0,256},{256,0},{1,257},{257,1},{2,258},{258,2},{3,259},{259,3},{4... | collective-permute-start | bytes 393224 | tf_op jit(solution)/shard_map/ppermute | solution.py:11
Sparse Core Ops, SparseCore 0:
  181.2 54.4 reduce-scatter.1
